TPU v7x, 256 devices: a whole 4x4x8 slice. The times are simulated.
256 devices in a mesh: tm: 128 (over z, y, x), rows: 2 (over core).
Axes of the slice: x: 4, y: 4, z: 8, core: 2. Of those that a mesh axis runs over, the one named last changes fastest.
Arguments:
- band_blocks: float32 [8, 3, 64, 64], replicated, may hold values from 0.1 to 1
- band_offsets: int32 [8, 3], replicated, may hold values from 0 to 7, as said below
- retention: float32 [512], replicated, may hold values from 0.85 to 0.99
- frame_scale: float32 [512, 8], P('tm'), may hold values from 0.95 to 0.999
- sensor_index: int32 [128], replicated, may hold values from 0 to 511, as said below
- sensor_gain: float32 [128], replicated, may hold values from 0.2 to 0.6
- readings: float32 [512, 128], P('tm'), may hold values from -6 to 6
- noise_cov: float32 [512, 512], P(None, 'rows'), may hold values from -0.01 to 0.2
- initial_mean: float32 [512], replicated, may hold values from -6 to 6
- smoother_gain: float32 [512, 512], replicated, may hold values from -0.001 to 1, as said below
Outputs:
- filtered_cov: float32 [128, 512, 512], P('tm', None, 'rows')
- smoothed_means: float32 [512, 512], P('tm', 'rows')
Inputs may be any that keep to these rules, and one draw needn't show every extreme that they name: `band_offsets`: band 0 of block row i names block i; the other bands of a row name distinct other blocks. `sensor_index`: the sensors read distinct nodes. Every eigenvalue of smoother_gain lies inside the unit circle.
All inputs are finite; a program needn't handle non-finite values.
Results may differ from a plain program's by a relative error of at most 0.0003.
Values sent between devices are 32-bit elements; how exact they have to be, the bound alone decides.
No kernel may reach another device: no remote copies, remote signals or barrier semaphores. Data moves between devices by JAX's collectives and lax.ppermute only.
A program may use at most 64 MiB of HBM per device.

v0:
```python
import jax
import jax.numpy as jnp
from jax import lax
from jax.sharding import PartitionSpec as P

HIGHEST_PRECISION = lax.Precision.HIGHEST


def shifted(value, axis, steps):
    count = lax.axis_size(axis)
    leading, last = (max(0, -steps), min(count, count - steps))
    return lax.ppermute(value, axis, [(source, source + steps) for source in range(leading, last)])


def matmul(left, right):
    return jnp.dot(left, right, precision=HIGHEST_PRECISION, preferred_element_type=jnp.float32)


def build_coupling(band_blocks, band_offsets, retention):
    block_count = band_blocks.shape[0]
    block_size = band_blocks.shape[2]
    totals = jnp.sum(band_blocks, axis=(1, 3))
    normed = band_blocks / totals[:, None, :, None]
    placement = (
        band_offsets[:, :, None] == jnp.arange(block_count, dtype=jnp.int32)[None, None, :]
    ).astype(jnp.float32)
    spread_matrix = jnp.einsum("ibj,ibac->iajc", placement, normed, precision=HIGHEST_PRECISION)
    spread_matrix = spread_matrix.reshape(block_count * block_size, block_count * block_size)
    return (1.0 - retention)[:, None] * spread_matrix + jnp.diag(retention)


def matrix_power(square, exponent):
    result = None
    factor = square
    while exponent > 0:
        if exponent % 2 == 1:
            result = factor
        exponent = exponent // 2
        if exponent > 0:
            factor = matmul(factor, factor)
    return result


def local(
    band_blocks,
    band_offsets,
    retention,
    frame_scale,
    sensor_index,
    sensor_gain,
    readings,
    noise_cov,
    initial_mean,
    smoother_gain,
):
    node_count = retention.shape[0]
    block_size = band_blocks.shape[2]
    frames = readings.shape[0]
    panel_width = noise_cov.shape[1]
    tm_devices = lax.axis_size("tm")
    segment = lax.axis_index("tm")
    panel_start = lax.axis_index("rows") * panel_width
    coupling = build_coupling(band_blocks, band_offsets, retention)
    sensor_hit = (sensor_index[:, None] == jnp.arange(node_count, dtype=jnp.int32)[None, :]).astype(
        jnp.float32
    )
    damping = 1.0 - matmul(sensor_gain, sensor_hit)
    inject = matmul(readings * sensor_gain[None, :], sensor_hit)
    anchor = jnp.where(segment == 0, initial_mean, jnp.zeros_like(initial_mean))

    def transition(frame):
        scale_row = lax.dynamic_index_in_dim(frame_scale, frame, 0, keepdims=False)
        return jnp.repeat(scale_row, block_size)[:, None] * coupling

    def injected(frame):
        return lax.dynamic_index_in_dim(inject, frame, 0, keepdims=False)

    first_update = damping[:, None] * transition(0)
    first_offset = matmul(first_update, anchor) + inject[0]
    columns = (
        jnp.arange(node_count, dtype=jnp.int32)[:, None]
        == panel_start + jnp.arange(panel_width, dtype=jnp.int32)[None, :]
    ).astype(jnp.float32)

    def segment_frame(frame, carry):
        chain_cols, offset, cov_cols = carry
        update = damping[:, None] * transition(frame)
        gathered = lax.all_gather(cov_cols, "rows", axis=1, tiled=True)
        update_rows = lax.dynamic_slice_in_dim(update, panel_start, panel_width, 0)
        cov_cols = matmul(update, matmul(gathered, update_rows.T)) + noise_cov
        return (matmul(update, chain_cols), matmul(update, offset) + injected(frame), cov_cols)

    element = lax.fori_loop(
        1, frames, segment_frame, (matmul(first_update, columns), first_offset, noise_cov)
    )

    def combine(succeeding, preceding):
        later_full, earlier_cov = (
            lax.all_gather(succeeding[0], "rows", axis=1, tiled=True),
            lax.all_gather(preceding[2], "rows", axis=1, tiled=True),
        )
        later_rows = lax.dynamic_slice_in_dim(later_full, panel_start, panel_width, 0)
        return (
            matmul(later_full, preceding[0]),
            matmul(later_full, preceding[1]) + succeeding[1],
            matmul(later_full, matmul(earlier_cov, later_rows.T)) + succeeding[2],
        )

    distances = [1] + [
        1 << level for level in range(tm_devices.bit_length()) if 1 << level < tm_devices
    ]
    prefix = element
    for position, stride in enumerate(distances):
        received = shifted((prefix[0], prefix[1], prefix[2]), "tm", stride)
        if position == 0:
            prefix = received
        else:
            merged = combine(prefix, received)
            prefix = tuple(
                (
                    jnp.where(segment >= stride, new_part, old_part)
                    for new_part, old_part in zip(merged, prefix)
                )
            )
    ending = combine(element, prefix)
    cov_out = ending[2][None]
    mean_start = jnp.where(segment == 0, initial_mean, prefix[1])

    def filter_frame(mean_now, frame):
        predicted = matmul(transition(frame), mean_now)
        mean_now = damping * predicted + injected(frame)
        return (mean_now, (mean_now, predicted))

    _, (mean_stack, pred_stack) = lax.scan(
        filter_frame, mean_start, jnp.arange(frames, dtype=jnp.int32)
    )

    def smooth_pass(bracket):

        def frame_back(bracket, inputs):
            mean_now, predicted = inputs
            smooth = mean_now + matmul(smoother_gain, bracket)
            return (smooth - predicted, smooth)

        return lax.scan(frame_back, bracket, (mean_stack, pred_stack), reverse=True)

    own_bracket, _ = smooth_pass(jnp.zeros_like(initial_mean))
    gain_power = matrix_power(smoother_gain, frames)
    suffix = own_bracket
    for position, stride in enumerate(distances):
        received = shifted(suffix, "tm", -stride)
        if position == 0:
            suffix = received
        else:
            suffix = suffix + matmul(gain_power, received)
            gain_power = matmul(gain_power, gain_power)
    _, smoothed = smooth_pass(suffix)
    return (cov_out, lax.dynamic_slice_in_dim(smoothed, panel_start, panel_width, 1))


def solution(mesh):
    return jax.shard_map(
        local,
        mesh=mesh,
        in_specs=(P(), P(), P(), P("tm", None), P(), P(), P("tm", None), P(None, "rows"), P(), P()),
        out_specs=(P("tm", None, "rows"), P("tm", "rows")),
        check_vma=False,
    )
```

profile of v0, /device:TPU:1, one launch (start us, length us, event | category | flops | bytes accessed | tf_op | source)
XLA Modules:
  0.0 583.1 jit_solution(16345871227725126471)
XLA Ops:
  18.0 73.0 %while.66 = (s32[]{:T(128)}, f32[512,256]{1,0:T(8,128)S(1)}, f32[512]{0:T(512)S(1)}, f32[512,256]{1,0:T(8,128)S(1)}, f32[512]{0:T(512)S(1)}, /*index=5*/f32[4,8]...) while((s32[]{:T(128)}, f32[512,256]{1,0:T(8,128)S(1)}, ...), condition=%wide.region_2.3_spmd, body=%wide.region_1.2_spmd.sunk | while | flops 2419720704 | bytes 17850712 | solution.py:93
  21.2 18.8 %all-gather.50.cloned.1.call-done = f32[512,512]{1,0:T(8,128)} async-done(((f32[512,256]{1,0:T(8,128)}), f32[512,512]{1,0:T(8,128)}) %all-gather.50.cloned.1.call-update) | async-done | bytes 1048592 | tf_op jit(solution)/shard_map/while/body/eval_jaxpr/all_gather | solution.py:88
  47.7 15.6 %all-gather.50.cloned.1.call-done = f32[512,512]{1,0:T(8,128)} async-done(((f32[512,256]{1,0:T(8,128)}), f32[512,512]{1,0:T(8,128)}) %all-gather.50.cloned.1.call-update) | async-done | bytes 1048592 | tf_op jit(solution)/shard_map/while/body/eval_jaxpr/all_gather | solution.py:88
  71.0 15.6 %all-gather.50.cloned.1.call-done = f32[512,512]{1,0:T(8,128)} async-done(((f32[512,256]{1,0:T(8,128)}), f32[512,512]{1,0:T(8,128)}) %all-gather.50.cloned.1.call-update) | async-done | bytes 1048592 | tf_op jit(solution)/shard_map/while/body/eval_jaxpr/all_gather | solution.py:88
  97.0 7.9 %collective-permute-done = f32[512,256]{1,0:T(8,128)S(1)} collective-permute-done((f32[512,256]{1,0:T(8,128)S(1)}, f32[512,256]{1,0:T(8,128)S(1)}, u32[]{:S(2)}, u32[]{:S(2)}) %collective-permute-start) | collective-permute-done | bytes 524320 | tf_op jit(solution)/shard_map/ppermute | solution.py:12
  105.8 10.4 %collective-permute-done.7 = f32[512,256]{1,0:T(8,128)S(1)} collective-permute-done((f32[512,256]{1,0:T(8,128)S(1)}, f32[512,256]{1,0:T(8,128)S(1)}, u32[]{:S(2)}, u32[]{:S(2)}) %collective-permute-start.7) | collective-permute-done | bytes 524320 | tf_op jit(solution)/shard_map/ppermute | solution.py:12
  120.3 10.2 %collective-permute-done.8 = f32[512,256]{1,0:T(8,128)S(1)} collective-permute-done((f32[512,256]{1,0:T(8,128)S(1)}, f32[512,256]{1,0:T(8,128)S(1)}, u32[]{:S(2)}, u32[]{:S(2)}) %collective-permute-start.8) | collective-permute-done | bytes 524320 | tf_op jit(solution)/shard_map/ppermute | solution.py:12
  135.5 9.6 %collective-permute-done.1 = f32[512,256]{1,0:T(8,128)S(1)} collective-permute-done((f32[512,256]{1,0:T(8,128)}, f32[512,256]{1,0:T(8,128)S(1)}, u32[]{:S(2)}, u32[]{:S(2)}) %collective-permute-start.1) | collective-permute-done | bytes 524320 | tf_op jit(solution)/shard_map/ppermute | solution.py:12
  165.2 10.2 %collective-permute-done.9 = f32[512,256]{1,0:T(8,128)} collective-permute-done((f32[512,256]{1,0:T(8,128)S(1)}, f32[512,256]{1,0:T(8,128)}, u32[]{:S(2)}, u32[]{:S(2)}) %collective-permute-start.9) | collective-permute-done | bytes 524320 | tf_op jit(solution)/shard_map/ppermute | solution.py:12
  182.1 9.4 %collective-permute-done.2 = f32[512,256]{1,0:T(8,128)} collective-permute-done((f32[512,256]{1,0:T(8,128)S(1)}, f32[512,256]{1,0:T(8,128)}, u32[]{:S(2)}, u32[]{:S(2)}) %collective-permute-start.2) | collective-permute-done | bytes 524320 | tf_op jit(solution)/shard_map/ppermute | solution.py:12
  194.7 9.0 %all-gather.36.cloned.1.call-done = f32[512,512]{1,0:T(8,128)} async-done(((f32[512,256]{1,0:T(8,128)}), f32[512,512]{1,0:T(8,128)}) %all-gather.36.cloned.1.call-update) | async-done | bytes 1048592 | tf_op jit(solution)/shard_map/all_gather | solution.py:100
  211.7 10.3 %collective-permute-done.10 = f32[512,256]{1,0:T(8,128)} collective-permute-done((f32[512,256]{1,0:T(8,128)S(1)}, f32[512,256]{1,0:T(8,128)}, u32[]{:S(2)}, u32[]{:S(2)}) %collective-permute-start.10) | collective-permute-done | bytes 524320 | tf_op jit(solution)/shard_map/ppermute | solution.py:12
  227.1 9.4 %collective-permute-done.3 = f32[512,256]{1,0:T(8,128)} collective-permute-done((f32[512,256]{1,0:T(8,128)S(1)}, f32[512,256]{1,0:T(8,128)}, u32[]{:S(2)}, u32[]{:S(2)}) %collective-permute-start.3) | collective-permute-done | bytes 524320 | tf_op jit(solution)/shard_map/ppermute | solution.py:12
  254.6 10.2 %collective-permute-done.11 = f32[512,256]{1,0:T(8,128)} collective-permute-done((f32[512,256]{1,0:T(8,128)S(1)}, f32[512,256]{1,0:T(8,128)}, u32[]{:S(2)}, u32[]{:S(2)}) %collective-permute-start.11) | collective-permute-done | bytes 524320 | tf_op jit(solution)/shard_map/ppermute | solution.py:12
  271.4 9.4 %collective-permute-done.4 = f32[512,256]{1,0:T(8,128)} collective-permute-done((f32[512,256]{1,0:T(8,128)S(1)}, f32[512,256]{1,0:T(8,128)}, u32[]{:S(2)}, u32[]{:S(2)}) %collective-permute-start.4) | collective-permute-done | bytes 524320 | tf_op jit(solution)/shard_map/ppermute | solution.py:12
  289.1 6.6 %collective-permute-start.12 = (f32[512,256]{1,0:T(8,128)S(1)}, f32[512,256]{1,0:T(8,128)}, u32[]{:S(2)}, u32[]{:S(2)}) collective-permute-start(f32[512,256]{1,0:T(8,128)S(1)} %fusion.11), channel_id=1, source_target_pairs={{0,32},{2,34},{4,36},{6,38},{8,40},{10,42},{12,44},{14,46},{16,48}... | collective-permute-start | bytes 1572872 | tf_op jit(solution)/shard_map/ppermute | solution.py:12
  295.6 8.5 %collective-permute-done.12 = f32[512,256]{1,0:T(8,128)} collective-permute-done((f32[512,256]{1,0:T(8,128)S(1)}, f32[512,256]{1,0:T(8,128)}, u32[]{:S(2)}, u32[]{:S(2)}) %collective-permute-start.12) | collective-permute-done | bytes 524320 | tf_op jit(solution)/shard_map/ppermute | solution.py:12
  309.3 7.7 %collective-permute-done.5 = f32[512,256]{1,0:T(8,128)} collective-permute-done((f32[512,256]{1,0:T(8,128)S(1)}, f32[512,256]{1,0:T(8,128)}, u32[]{:S(2)}, u32[]{:S(2)}) %collective-permute-start.5) | collective-permute-done | bytes 524320 | tf_op jit(solution)/shard_map/ppermute | solution.py:12
  346.3 29.4 %collective-permute-start.6 = (f32[512,256]{1,0:T(8,128)S(1)}, f32[512,256]{1,0:T(8,128)S(1)}, u32[]{:S(2)}, u32[]{:S(2)}) collective-permute-start(f32[512,256]{1,0:T(8,128)S(1)} %copy-done.13), channel_id=1, source_target_pairs={{0,64},{2,66},{4,68},{6,70},{8,72},{10,74},{12,76},{14,78},{16,80}... | collective-permute-start | bytes 1572872 | tf_op jit(solution)/shard_map/ppermute | solution.py:12
  392.9 15.9 %collective-permute-start.14 = (f32[512,256]{1,0:T(8,128)S(1)}, f32[512,256]{1,0:T(8,128)}, u32[]{:S(2)}, u32[]{:S(2)}) collective-permute-start(f32[512,256]{1,0:T(8,128)S(1)} %fusion.9), channel_id=1, source_target_pairs={{0,128},{2,130},{4,132},{6,134},{8,136},{10,138},{12,140},{14,142}... | collective-permute-start | bytes 1572872 | tf_op jit(solution)/shard_map/ppermute | solution.py:12
  421.1 16.1 %collective-permute-start.21 = (f32[512]{0:T(512)S(1)}, f32[512]{0:T(512)S(1)}, u32[]{:S(2)}, u32[]{:S(2)}) collective-permute-start(f32[512]{0:T(512)S(1)} %add_select_fusion.2), channel_id=1, source_target_pairs={{0,64},{2,66},{4,68},{6,70},{8,72},{10,74},{12,76},{14,78},{16,80}... | collective-permute-start | bytes 6152 | tf_op jit(solution)/shard_map/ppermute | solution.py:12
  440.2 8.2 %collective-permute-start.22 = (f32[512]{0:T(512)S(1)}, f32[512]{0:T(512)S(1)}, u32[]{:S(2)}, u32[]{:S(2)}) collective-permute-start(f32[512]{0:T(512)S(1)} %add_select_fusion.1), channel_id=1, source_target_pairs={{0,128},{2,130},{4,132},{6,134},{8,136},{10,138},{12,140},{14,142}... | collective-permute-start | bytes 6152 | tf_op jit(solution)/shard_map/ppermute | solution.py:12
  451.4 15.8 %while.67 = (s32[]{:T(128)}, f32[512]{0:T(512)S(1)}, f32[4,512]{1,0:T(4,128)S(1)}, f32[4,512]{1,0:T(4,128)S(1)}, s32[4]{0:T(128)S(1)}, /*index=5*/f32[4,8]{1,0:T...) while((s32[]{:T(128)}, f32[512]{0:T(512)S(1)}, ...), condition=%wide.region_4.5_spmd, body=%wide.region_3.4_spmd.sunk | while | flops 3408901 | bytes 1081619 | solution.py:134
  537.5 33.6 %all-gather.48.cloned.1.call-done = f32[512,512]{1,0:T(8,128)} async-done(((f32[512,256]{1,0:T(8,128)}), f32[512,512]{1,0:T(8,128)}) %all-gather.48.cloned.1.call-update) | async-done | bytes 1048592 | tf_op jit(solution)/shard_map/all_gather | solution.py:100
  (368 shorter events, 284.1 us)
Async XLA Ops:
  18.0 22.1 %all-gather.50.cloned.1.call-start = ((), (), s32[]{:S(2)}) async-start(), calls=%async_computation.16 | async-start | bytes 1572864 | tf_op jit(solution)/shard_map/while/body/eval_jaxpr/all_gather | solution.py:88
  44.5 18.9 %all-gather.50.cloned.1.call-start = ((), (), s32[]{:S(2)}) async-start(), calls=%async_computation.16 | async-start | bytes 1572864 | tf_op jit(solution)/shard_map/while/body/eval_jaxpr/all_gather | solution.py:88
  67.7 18.9 %all-gather.50.cloned.1.call-start = ((), (), s32[]{:S(2)}) async-start(), calls=%async_computation.16 | async-start | bytes 1572864 | tf_op jit(solution)/shard_map/while/body/eval_jaxpr/all_gather | solution.py:88
  91.0 54.9 %all-gather.20.cloned.1.call-start = ((), (), s32[]{:S(2)}) async-start(), calls=%async_computation.1 | async-start | bytes 1572864 | tf_op jit(solution)/shard_map/all_gather | solution.py:99
  93.9 22.2 %collective-permute-start.7 = (f32[512,256]{1,0:T(8,128)S(1)}, f32[512,256]{1,0:T(8,128)S(1)}, u32[]{:S(2)}, u32[]{:S(2)}) collective-permute-start(f32[512,256]{1,0:T(8,128)S(1)} %get-tuple-element.586), channel_id=1, source_target_pairs={{0,2},{2,4},{4,6},{6,8},{8,10},{10,12},{12,14},{14,16},{16,18},{18... | collective-permute-start | bytes 1572872 | tf_op jit(solution)/shard_map/ppermute | solution.py:12
  105.8 50.2 %all-gather.34.cloned.1.call-start = ((), (), s32[]{:S(2)}) async-start(), calls=%async_computation.8 | async-start | bytes 1572864 | tf_op jit(solution)/shard_map/all_gather | solution.py:100
  131.3 60.2 %all-gather.22.cloned.1.call-start = ((), (), s32[]{:S(2)}) async-start(), calls=%async_computation.2 | async-start | bytes 1572864 | tf_op jit(solution)/shard_map/all_gather | solution.py:99
  149.3 54.4 %all-gather.36.cloned.1.call-start = ((), (), s32[]{:S(2)}) async-start(), calls=%async_computation.9 | async-start | bytes 1572864 | tf_op jit(solution)/shard_map/all_gather | solution.py:100
  175.5 61.0 %all-gather.24.cloned.1.call-start = ((), (), s32[]{:S(2)}) async-start(), calls=%async_computation.3 | async-start | bytes 1572864 | tf_op jit(solution)/shard_map/all_gather | solution.py:99
  194.6 50.3 %all-gather.38.cloned.1.call-start = ((), (), s32[]{:S(2)}) async-start(), calls=%async_computation.10 | async-start | bytes 1572864 | tf_op jit(solution)/shard_map/all_gather | solution.py:100
  222.0 58.8 %all-gather.26.cloned.1.call-start = ((), (), s32[]{:S(2)}) async-start(), calls=%async_computation.4 | async-start | bytes 1572864 | tf_op jit(solution)/shard_map/all_gather | solution.py:99
  239.7 45.1 %all-gather.40.cloned.1.call-start = ((), (), s32[]{:S(2)}) async-start(), calls=%async_computation.11 | async-start | bytes 1572864 | tf_op jit(solution)/shard_map/all_gather | solution.py:100
  264.8 52.2 %all-gather.28.cloned.1.call-start = ((), (), s32[]{:S(2)}) async-start(), calls=%async_computation.5 | async-start | bytes 1572864 | tf_op jit(solution)/shard_map/all_gather | solution.py:99
  284.1 41.8 %all-gather.42.cloned.1.call-start = ((), (), s32[]{:S(2)}) async-start(), calls=%async_computation.12 | async-start | bytes 1572864 | tf_op jit(solution)/shard_map/all_gather | solution.py:100
  304.2 80.8 %all-gather.30.cloned.1.call-start = ((), (), s32[]{:S(2)}) async-start(), calls=%async_computation.6 | async-start | bytes 1572864 | tf_op jit(solution)/shard_map/all_gather | solution.py:99
  320.1 68.0 %all-gather.44.cloned.1.call-start = ((), (), s32[]{:S(2)}) async-start(), calls=%async_computation.13 | async-start | bytes 1572864 | tf_op jit(solution)/shard_map/all_gather | solution.py:100
  345.2 103.9 %all-gather.32.cloned.1.call-start = ((), (), s32[]{:S(2)}) async-start(), calls=%async_computation.7 | async-start | bytes 1572864 | tf_op jit(solution)/shard_map/all_gather | solution.py:99
  346.3 38.8 %collective-permute-start.6 = (f32[512,256]{1,0:T(8,128)S(1)}, f32[512,256]{1,0:T(8,128)S(1)}, u32[]{:S(2)}, u32[]{:S(2)}) collective-permute-start(f32[512,256]{1,0:T(8,128)S(1)} %copy-done.13), channel_id=1, source_target_pairs={{0,64},{2,66},{4,68},{6,70},{8,72},{10,74},{12,76},{14,78},{16,80}... | collective-permute-start | bytes 1572872 | tf_op jit(solution)/shard_map/ppermute | solution.py:12
  380.0 28.8 %collective-permute-start.18 = (f32[512]{0:T(512)S(1)}, f32[512]{0:T(512)S(1)}, u32[]{:S(2)}, u32[]{:S(2)}) collective-permute-start(f32[512]{0:T(512)S(1)} %add_select_fusion.5), channel_id=1, source_target_pairs={{0,8},{2,10},{4,12},{6,14},{8,16},{10,18},{12,20},{14,22},{16,24},... | collective-permute-start | bytes 6152 | tf_op jit(solution)/shard_map/ppermute | solution.py:12
  388.1 140.4 %all-gather.46.cloned.1.call-start = ((), (), s32[]{:S(2)}) async-start(), calls=%async_computation.14 | async-start | bytes 1572864 | tf_op jit(solution)/shard_map/all_gather | solution.py:100
  392.9 23.9 %collective-permute-start.14 = (f32[512,256]{1,0:T(8,128)S(1)}, f32[512,256]{1,0:T(8,128)}, u32[]{:S(2)}, u32[]{:S(2)}) collective-permute-start(f32[512,256]{1,0:T(8,128)S(1)} %fusion.9), channel_id=1, source_target_pairs={{0,128},{2,130},{4,132},{6,134},{8,136},{10,138},{12,140},{14,142}... | collective-permute-start | bytes 1572872 | tf_op jit(solution)/shard_map/ppermute | solution.py:12
  416.8 120.7 %all-gather.18.cloned.1.call-start = ((), (), s32[]{:S(2)}) async-start(), calls=%async_computation | async-start | bytes 1572864 | tf_op jit(solution)/shard_map/all_gather | solution.py:99
  421.1 16.9 %collective-permute-start.21 = (f32[512]{0:T(512)S(1)}, f32[512]{0:T(512)S(1)}, u32[]{:S(2)}, u32[]{:S(2)}) collective-permute-start(f32[512]{0:T(512)S(1)} %add_select_fusion.2), channel_id=1, source_target_pairs={{0,64},{2,66},{4,68},{6,70},{8,72},{10,74},{12,76},{14,78},{16,80}... | collective-permute-start | bytes 6152 | tf_op jit(solution)/shard_map/ppermute | solution.py:12
  448.4 122.8 %all-gather.48.cloned.1.call-start = ((), (), s32[]{:S(2)}) async-start(), calls=%async_computation.15 | async-start | bytes 1572864 | tf_op jit(solution)/shard_map/all_gather | solution.py:100
  (68 other events, 587.3 us)
Sparse Core Ops, SparseCore 0:
  21.2 18.8 all-gather.49
  47.7 15.6 all-gather.49
  70.9 15.6 all-gather.49
Sparse Core Ops, SparseCore 1:
  105.8 18.9 all-gather.19
  131.4 24.5 all-gather.33
  157.6 22.3 all-gather.21
  181.8 21.9 all-gather.35
  205.5 19.8 all-gather.23
  227.2 17.7 all-gather.37
  246.7 16.0 all-gather.25
  264.9 19.8 all-gather.39
  286.4 18.9 all-gather.27
  307.2 18.6 all-gather.41
  327.5 16.3 all-gather.29
  345.6 36.4 all-gather.43
  388.2 24.7 all-gather.31
  416.9 26.1 all-gather.45
  448.5 15.5 all-gather.17
  532.7 38.4 all-gather.47
where the time goes:
time: 593 us; the launch traced here: 583 us
  waiting for transfers between devices  261 us (44%)
  starting transfers between devices  157 us (26%)
  matrix products  120 us (20%)
  between operations  17 us (3%)
  local copies, waits for them, and re-layouts  15.7 us (3%)
  loops' own time  8.32 us (1%)
    ppermute x31, starting transfers between devices, shifted(): lax.ppermute(value, axis, [(source, source + steps) for source in range(l...  155 us
    ppermute x31, waiting for transfers between devices, shifted(): lax.ppermute(value, axis, [(source, source + steps) for source in range(l...  150 us
    dot_general x72, matrix products, matmul(): jnp.dot(left, right, precision=HIGHEST_PRECISION, preferred_element_type=...  118 us
    all_gather x8, waiting for transfers between devices, combine(): lax.all_gather(preceding[2], 'rows', axis=1, tiled=True)  60.2 us
    all_gather x3, waiting for transfers between devices, segment_frame(): gathered = lax.all_gather(cov_cols, 'rows', axis=1, tiled=True)  50.1 us
  transfers between devices with their start and end apart: 50, of which 38 were waited for; matrix products, arithmetic and copies ran while one was open for 18% of the time, Pallas kernels for 0%

commit v1 on v0

--- a/solution.py
+++ b/solution.py
@@ -85,7 +85,9 @@
     def segment_frame(frame, carry):
         chain_cols, offset, cov_cols = carry
         update = damping[:, None] * transition(frame)
-        gathered = lax.all_gather(cov_cols, "rows", axis=1, tiled=True)
+        gathered = jnp.concatenate(
+            lax.all_to_all(jnp.stack([cov_cols] * lax.axis_size("rows")), "rows", 0, 0), axis=1
+        )
         update_rows = lax.dynamic_slice_in_dim(update, panel_start, panel_width, 0)
         cov_cols = matmul(update, matmul(gathered, update_rows.T)) + noise_cov
         return (matmul(update, chain_cols), matmul(update, offset) + injected(frame), cov_cols)

time: 593 us -> 563 us (0.949)
  waiting for transfers between devices: 261 us -> 216 us
  starting transfers between devices: 157 us -> 167 us
    all_gather x3 -> x0, waiting for transfers between devices: 50.1 us -> none  [segment_frame(): gathered = lax.all_gather(cov_cols, 'rows', axis=1, tiled=True)]
    all_to_all x0 -> x3, starting transfers between devices: none -> 14 us  [segment_frame(): lax.all_to_all(jnp.stack([cov_cols] * lax.axis_size('rows')), 'rows', 0, 0)]
  transfers between devices with their start and end apart: 50 -> 50, of which waited for: 38 -> 34; matrix products, arithmetic and copies ran while one was open for 18% -> 19% of each run, Pallas kernels for 0% -> 0%
where the time goes in v1:
time: 563 us; the launch traced here: 553 us
  waiting for transfers between devices  216 us (38%)
  starting transfers between devices  167 us (30%)
  matrix products  118 us (21%)
  local copies, waits for them, and re-layouts  21.5 us (4%)
  between operations  15.3 us (3%)
  other arithmetic  8.25 us (1%)
  loops' own time  7.39 us (1%)
    ppermute x31, waiting for transfers between devices, shifted(): lax.ppermute(value, axis, [(source, source + steps) for source in range(l...  155 us
    ppermute x31, starting transfers between devices, shifted(): lax.ppermute(value, axis, [(source, source + steps) for source in range(l...  151 us
    dot_general x72, matrix products, matmul(): jnp.dot(left, right, precision=HIGHEST_PRECISION, preferred_element_type=...  116 us
    all_gather x8, waiting for transfers between devices, combine(): lax.all_gather(preceding[2], 'rows', axis=1, tiled=True)  60.9 us
    all_to_all x3, starting transfers between devices, segment_frame(): lax.all_to_all(jnp.stack([cov_cols] * lax.axis_size('rows')), 'rows', 0, 0)  14 us
  transfers between devices with their start and end apart: 50, of which 34 were waited for; matrix products, arithmetic and copies ran while one was open for 19% of the time, Pallas kernels for 0%

profile of v1, /device:TPU:1, one launch (start us, length us, event | category | flops | bytes accessed | tf_op | source)
XLA Modules:
  0.0 553.2 jit_solution(16045541849283404261)
XLA Ops:
  18.7 44.5 %while.66 = (s32[]{:T(128)}, f32[512,256]{1,0:T(8,128)}, f32[512]{0:T(512)S(1)}, f32[512,256]{1,0:T(8,128)}, f32[512]{0:T(512)S(1)}, /*index=5*/f32[4,8]{1,0:T(4...) while((s32[]{:T(128)}, f32[512,256]{1,0:T(8,128)}, ...), condition=%wide.region_2.3_spmd, body=%wide.region_1.2_spmd.sunk | while | flops 2419982848 | bytes 18899280 | solution.py:95
  21.1 6.8 %all-to-all-start = ((f32[2,512,256]{1,2,0:T(8,128)}), f32[2,512,256]{1,2,0:T(8,128)S(1)}, u32[]{:S(2)}, u32[]{:S(2)}) async-start(f32[2,512,256]{1,2,0:T(8,128)} %pad_maximum_fusion.2), calls=%async_computation | async-start | bytes 2097152 | tf_op jit(solution)/shard_map/while/body/eval_jaxpr/all_to_all | solution.py:89
  67.8 8.4 %collective-permute-done = f32[512,256]{1,0:T(8,128)S(1)} collective-permute-done((f32[512,256]{1,0:T(8,128)}, f32[512,256]{1,0:T(8,128)S(1)}, u32[]{:S(2)}, u32[]{:S(2)}) %collective-permute-start) | collective-permute-done | bytes 524320 | tf_op jit(solution)/shard_map/ppermute | solution.py:12
  77.0 10.4 %collective-permute-done.7 = f32[512,256]{1,0:T(8,128)S(1)} collective-permute-done((f32[512,256]{1,0:T(8,128)}, f32[512,256]{1,0:T(8,128)S(1)}, u32[]{:S(2)}, u32[]{:S(2)}) %collective-permute-start.7) | collective-permute-done | bytes 524320 | tf_op jit(solution)/shard_map/ppermute | solution.py:12
  91.4 10.3 %collective-permute-done.8 = f32[512,256]{1,0:T(8,128)S(1)} collective-permute-done((f32[512,256]{1,0:T(8,128)S(1)}, f32[512,256]{1,0:T(8,128)S(1)}, u32[]{:S(2)}, u32[]{:S(2)}) %collective-permute-start.8) | collective-permute-done | bytes 524320 | tf_op jit(solution)/shard_map/ppermute | solution.py:12
  106.8 9.8 %collective-permute-done.1 = f32[512,256]{1,0:T(8,128)S(1)} collective-permute-done((f32[512,256]{1,0:T(8,128)}, f32[512,256]{1,0:T(8,128)S(1)}, u32[]{:S(2)}, u32[]{:S(2)}) %collective-permute-start.1) | collective-permute-done | bytes 524320 | tf_op jit(solution)/shard_map/ppermute | solution.py:12
  120.1 8.5 %all-gather.33.cloned.1.call-done = f32[512,512]{1,0:T(8,128)} async-done(((f32[512,256]{1,0:T(8,128)}), f32[512,512]{1,0:T(8,128)}) %all-gather.33.cloned.1.call-update) | async-done | bytes 1048592 | tf_op jit(solution)/shard_map/all_gather | solution.py:102
  137.0 11.0 %collective-permute-done.9 = f32[512,256]{1,0:T(8,128)S(1)} collective-permute-done((f32[512,256]{1,0:T(8,128)S(1)}, f32[512,256]{1,0:T(8,128)S(1)}, u32[]{:S(2)}, u32[]{:S(2)}) %collective-permute-start.9) | collective-permute-done | bytes 524320 | tf_op jit(solution)/shard_map/ppermute | solution.py:12
  154.6 10.2 %collective-permute-done.2 = f32[512,256]{1,0:T(8,128)S(1)} collective-permute-done((f32[512,256]{1,0:T(8,128)S(1)}, f32[512,256]{1,0:T(8,128)S(1)}, u32[]{:S(2)}, u32[]{:S(2)}) %collective-permute-start.2) | collective-permute-done | bytes 524320 | tf_op jit(solution)/shard_map/ppermute | solution.py:12
  169.1 7.4 %all-gather.35.cloned.1.call-done = f32[512,512]{1,0:T(8,128)} async-done(((f32[512,256]{1,0:T(8,128)}), f32[512,512]{1,0:T(8,128)}) %all-gather.35.cloned.1.call-update) | async-done | bytes 1048592 | tf_op jit(solution)/shard_map/all_gather | solution.py:102
  184.3 10.2 %collective-permute-done.10 = f32[512,256]{1,0:T(8,128)} collective-permute-done((f32[512,256]{1,0:T(8,128)S(1)}, f32[512,256]{1,0:T(8,128)}, u32[]{:S(2)}, u32[]{:S(2)}) %collective-permute-start.10) | collective-permute-done | bytes 524320 | tf_op jit(solution)/shard_map/ppermute | solution.py:12
  199.6 9.7 %collective-permute-done.3 = f32[512,256]{1,0:T(8,128)} collective-permute-done((f32[512,256]{1,0:T(8,128)}, f32[512,256]{1,0:T(8,128)}, u32[]{:S(2)}, u32[]{:S(2)}) %collective-permute-start.3) | collective-permute-done | bytes 524320 | tf_op jit(solution)/shard_map/ppermute | solution.py:12
  228.2 10.2 %collective-permute-done.11 = f32[512,256]{1,0:T(8,128)} collective-permute-done((f32[512,256]{1,0:T(8,128)S(1)}, f32[512,256]{1,0:T(8,128)}, u32[]{:S(2)}, u32[]{:S(2)}) %collective-permute-start.11) | collective-permute-done | bytes 524320 | tf_op jit(solution)/shard_map/ppermute | solution.py:12
  238.5 6.5 %collective-permute-start.4 = (f32[512,256]{1,0:T(8,128)}, f32[512,256]{1,0:T(8,128)}, u32[]{:S(2)}, u32[]{:S(2)}) collective-permute-start(f32[512,256]{1,0:T(8,128)} %convolution_select_fusion.3), channel_id=1, source_target_pairs={{0,16},{2,18},{4,20},{6,22},{8,24},{10,26},{12,28},{14,30},{16,32}... | collective-permute-start | bytes 1572872 | tf_op jit(solution)/shard_map/ppermute | solution.py:12
  245.0 9.7 %collective-permute-done.4 = f32[512,256]{1,0:T(8,128)} collective-permute-done((f32[512,256]{1,0:T(8,128)}, f32[512,256]{1,0:T(8,128)}, u32[]{:S(2)}, u32[]{:S(2)}) %collective-permute-start.4) | collective-permute-done | bytes 524320 | tf_op jit(solution)/shard_map/ppermute | solution.py:12
  263.0 6.5 %collective-permute-start.12 = (f32[512,256]{1,0:T(8,128)S(1)}, f32[512,256]{1,0:T(8,128)}, u32[]{:S(2)}, u32[]{:S(2)}) collective-permute-start(f32[512,256]{1,0:T(8,128)S(1)} %fusion.11), channel_id=1, source_target_pairs={{0,32},{2,34},{4,36},{6,38},{8,40},{10,42},{12,44},{14,46},{16,48}... | collective-permute-start | bytes 1572872 | tf_op jit(solution)/shard_map/ppermute | solution.py:12
  269.5 8.5 %collective-permute-done.12 = f32[512,256]{1,0:T(8,128)} collective-permute-done((f32[512,256]{1,0:T(8,128)S(1)}, f32[512,256]{1,0:T(8,128)}, u32[]{:S(2)}, u32[]{:S(2)}) %collective-permute-start.12) | collective-permute-done | bytes 524320 | tf_op jit(solution)/shard_map/ppermute | solution.py:12
  283.1 8.0 %collective-permute-done.5 = f32[512,256]{1,0:T(8,128)} collective-permute-done((f32[512,256]{1,0:T(8,128)}, f32[512,256]{1,0:T(8,128)}, u32[]{:S(2)}, u32[]{:S(2)}) %collective-permute-start.5) | collective-permute-done | bytes 524320 | tf_op jit(solution)/shard_map/ppermute | solution.py:12
  320.3 29.6 %collective-permute-start.6 = (f32[512,256]{1,0:T(8,128)}, f32[512,256]{1,0:T(8,128)S(1)}, u32[]{:S(2)}, u32[]{:S(2)}) collective-permute-start(f32[512,256]{1,0:T(8,128)} %convolution_select_fusion.1), channel_id=1, source_target_pairs={{0,64},{2,66},{4,68},{6,70},{8,72},{10,74},{12,76},{14,78},{16,80}... | collective-permute-start | bytes 1572872 | tf_op jit(solution)/shard_map/ppermute | solution.py:12
  367.8 14.1 %collective-permute-start.14 = (f32[512,256]{1,0:T(8,128)S(1)}, f32[512,256]{1,0:T(8,128)}, u32[]{:S(2)}, u32[]{:S(2)}) collective-permute-start(f32[512,256]{1,0:T(8,128)S(1)} %fusion.9), channel_id=1, source_target_pairs={{0,128},{2,130},{4,132},{6,134},{8,136},{10,138},{12,140},{14,142}... | collective-permute-start | bytes 1572872 | tf_op jit(solution)/shard_map/ppermute | solution.py:12
  395.2 13.9 %collective-permute-start.21 = (f32[512]{0:T(512)S(1)}, f32[512]{0:T(512)S(1)}, u32[]{:S(2)}, u32[]{:S(2)}) collective-permute-start(f32[512]{0:T(512)S(1)} %add_select_fusion.2), channel_id=1, source_target_pairs={{0,64},{2,66},{4,68},{6,70},{8,72},{10,74},{12,76},{14,78},{16,80}... | collective-permute-start | bytes 6152 | tf_op jit(solution)/shard_map/ppermute | solution.py:12
  412.0 8.1 %collective-permute-start.22 = (f32[512]{0:T(512)S(1)}, f32[512]{0:T(512)S(1)}, u32[]{:S(2)}, u32[]{:S(2)}) collective-permute-start(f32[512]{0:T(512)S(1)} %add_select_fusion.1), channel_id=1, source_target_pairs={{0,128},{2,130},{4,132},{6,134},{8,136},{10,138},{12,140},{14,142}... | collective-permute-start | bytes 6152 | tf_op jit(solution)/shard_map/ppermute | solution.py:12
  423.2 14.8 %while.67 = (s32[]{:T(128)}, f32[512]{0:T(512)S(1)}, f32[4,512]{1,0:T(4,128)S(1)}, f32[4,512]{1,0:T(4,128)S(1)}, s32[4]{0:T(128)S(1)}, /*index=5*/f32[4,8]{1,0:T...) while((s32[]{:T(128)}, f32[512]{0:T(512)S(1)}, ...), condition=%wide.region_4.5_spmd, body=%wide.region_3.4_spmd.sunk | while | flops 3408901 | bytes 1081619 | solution.py:136
  507.5 33.6 %all-gather.47.cloned.1.call-done = f32[512,512]{1,0:T(8,128)} async-done(((f32[512,256]{1,0:T(8,128)}), f32[512,512]{1,0:T(8,128)}) %all-gather.47.cloned.1.call-update) | async-done | bytes 1048592 | tf_op jit(solution)/shard_map/all_gather | solution.py:102
  (367 shorter events, 287.7 us)
Async XLA Ops:
  7.2 109.4 %all-gather.19.cloned.1.call-start = ((), (), s32[]{:S(2)}) async-start(), calls=%async_computation.2 | async-start | bytes 1572864 | tf_op jit(solution)/shard_map/all_gather | solution.py:101
  64.6 22.7 %collective-permute-start.7 = (f32[512,256]{1,0:T(8,128)}, f32[512,256]{1,0:T(8,128)S(1)}, u32[]{:S(2)}, u32[]{:S(2)}) collective-permute-start(f32[512,256]{1,0:T(8,128)} %get-tuple-element.586), channel_id=1, source_target_pairs={{0,2},{2,4},{4,6},{6,8},{8,10},{10,12},{12,14},{14,16},{16,18},{18... | collective-permute-start | bytes 1572872 | tf_op jit(solution)/shard_map/ppermute | solution.py:12
  77.0 51.7 %all-gather.33.cloned.1.call-start = ((), (), s32[]{:S(2)}) async-start(), calls=%async_computation.9 | async-start | bytes 1572864 | tf_op jit(solution)/shard_map/all_gather | solution.py:102
  102.6 63.0 %all-gather.21.cloned.1.call-start = ((), (), s32[]{:S(2)}) async-start(), calls=%async_computation.3 | async-start | bytes 1572864 | tf_op jit(solution)/shard_map/all_gather | solution.py:101
  119.9 56.6 %all-gather.35.cloned.1.call-start = ((), (), s32[]{:S(2)}) async-start(), calls=%async_computation.10 | async-start | bytes 1572864 | tf_op jit(solution)/shard_map/all_gather | solution.py:102
  132.7 15.4 %collective-permute-start.9 = (f32[512,256]{1,0:T(8,128)S(1)}, f32[512,256]{1,0:T(8,128)S(1)}, u32[]{:S(2)}, u32[]{:S(2)}) collective-permute-start(f32[512,256]{1,0:T(8,128)S(1)} %fusion.14), channel_id=1, source_target_pairs={{0,4},{2,6},{4,8},{6,10},{8,12},{10,14},{12,16},{14,18},{16,20},{1... | collective-permute-start | bytes 1572872 | tf_op jit(solution)/shard_map/ppermute | solution.py:12
  148.9 60.4 %all-gather.23.cloned.1.call-start = ((), (), s32[]{:S(2)}) async-start(), calls=%async_computation.4 | async-start | bytes 1572864 | tf_op jit(solution)/shard_map/all_gather | solution.py:101
  148.9 15.8 %collective-permute-start.2 = (f32[512,256]{1,0:T(8,128)S(1)}, f32[512,256]{1,0:T(8,128)S(1)}, u32[]{:S(2)}, u32[]{:S(2)}) collective-permute-start(f32[512,256]{1,0:T(8,128)S(1)} %copy-done.14), channel_id=1, source_target_pairs={{0,4},{2,6},{4,8},{6,10},{8,12},{10,14},{12,16},{14,18},{16,20},{1... | collective-permute-start | bytes 1572872 | tf_op jit(solution)/shard_map/ppermute | solution.py:12
  169.0 49.7 %all-gather.37.cloned.1.call-start = ((), (), s32[]{:S(2)}) async-start(), calls=%async_computation.11 | async-start | bytes 1572864 | tf_op jit(solution)/shard_map/all_gather | solution.py:102
  194.5 60.2 %all-gather.25.cloned.1.call-start = ((), (), s32[]{:S(2)}) async-start(), calls=%async_computation.5 | async-start | bytes 1572864 | tf_op jit(solution)/shard_map/all_gather | solution.py:101
  212.7 46.0 %all-gather.39.cloned.1.call-start = ((), (), s32[]{:S(2)}) async-start(), calls=%async_computation.12 | async-start | bytes 1572864 | tf_op jit(solution)/shard_map/all_gather | solution.py:102
  223.0 15.4 %collective-permute-start.11 = (f32[512,256]{1,0:T(8,128)S(1)}, f32[512,256]{1,0:T(8,128)}, u32[]{:S(2)}, u32[]{:S(2)}) collective-permute-start(f32[512,256]{1,0:T(8,128)S(1)} %fusion.12), channel_id=1, source_target_pairs={{0,16},{2,18},{4,20},{6,22},{8,24},{10,26},{12,28},{14,30},{16,32}... | collective-permute-start | bytes 1572872 | tf_op jit(solution)/shard_map/ppermute | solution.py:12
  238.5 52.6 %all-gather.27.cloned.1.call-start = ((), (), s32[]{:S(2)}) async-start(), calls=%async_computation.6 | async-start | bytes 1572864 | tf_op jit(solution)/shard_map/all_gather | solution.py:101
  238.5 16.2 %collective-permute-start.4 = (f32[512,256]{1,0:T(8,128)}, f32[512,256]{1,0:T(8,128)}, u32[]{:S(2)}, u32[]{:S(2)}) collective-permute-start(f32[512,256]{1,0:T(8,128)} %convolution_select_fusion.3), channel_id=1, source_target_pairs={{0,16},{2,18},{4,20},{6,22},{8,24},{10,26},{12,28},{14,30},{16,32}... | collective-permute-start | bytes 1572872 | tf_op jit(solution)/shard_map/ppermute | solution.py:12
  258.2 41.6 %all-gather.41.cloned.1.call-start = ((), (), s32[]{:S(2)}) async-start(), calls=%async_computation.13 | async-start | bytes 1572864 | tf_op jit(solution)/shard_map/all_gather | solution.py:102
  278.1 81.7 %all-gather.29.cloned.1.call-start = ((), (), s32[]{:S(2)}) async-start(), calls=%async_computation.7 | async-start | bytes 1572864 | tf_op jit(solution)/shard_map/all_gather | solution.py:101
  294.5 68.7 %all-gather.43.cloned.1.call-start = ((), (), s32[]{:S(2)}) async-start(), calls=%async_computation.14 | async-start | bytes 1572864 | tf_op jit(solution)/shard_map/all_gather | solution.py:102
  319.3 101.6 %all-gather.31.cloned.1.call-start = ((), (), s32[]{:S(2)}) async-start(), calls=%async_computation.8 | async-start | bytes 1572864 | tf_op jit(solution)/shard_map/all_gather | solution.py:101
  320.3 39.5 %collective-permute-start.6 = (f32[512,256]{1,0:T(8,128)}, f32[512,256]{1,0:T(8,128)S(1)}, u32[]{:S(2)}, u32[]{:S(2)}) collective-permute-start(f32[512,256]{1,0:T(8,128)} %convolution_select_fusion.1), channel_id=1, source_target_pairs={{0,64},{2,66},{4,68},{6,70},{8,72},{10,74},{12,76},{14,78},{16,80}... | collective-permute-start | bytes 1572872 | tf_op jit(solution)/shard_map/ppermute | solution.py:12
  352.9 29.0 %collective-permute-start.18 = (f32[512]{0:T(512)S(1)}, f32[512]{0:T(512)S(1)}, u32[]{:S(2)}, u32[]{:S(2)}) collective-permute-start(f32[512]{0:T(512)S(1)} %add_select_fusion.5), channel_id=1, source_target_pairs={{0,8},{2,10},{4,12},{6,14},{8,16},{10,18},{12,20},{14,22},{16,24},... | collective-permute-start | bytes 6152 | tf_op jit(solution)/shard_map/ppermute | solution.py:12
  363.1 135.3 %all-gather.45.cloned.1.call-start = ((), (), s32[]{:S(2)}) async-start(), calls=%async_computation.15 | async-start | bytes 1572864 | tf_op jit(solution)/shard_map/all_gather | solution.py:102
  367.8 20.7 %collective-permute-start.14 = (f32[512,256]{1,0:T(8,128)S(1)}, f32[512,256]{1,0:T(8,128)}, u32[]{:S(2)}, u32[]{:S(2)}) collective-permute-start(f32[512,256]{1,0:T(8,128)S(1)} %fusion.9), channel_id=1, source_target_pairs={{0,128},{2,130},{4,132},{6,134},{8,136},{10,138},{12,140},{14,142}... | collective-permute-start | bytes 1572872 | tf_op jit(solution)/shard_map/ppermute | solution.py:12
  388.6 118.9 %all-gather.17.cloned.1.call-start = ((), (), s32[]{:S(2)}) async-start(), calls=%async_computation.1 | async-start | bytes 1572864 | tf_op jit(solution)/shard_map/all_gather | solution.py:101
  420.2 120.9 %all-gather.47.cloned.1.call-start = ((), (), s32[]{:S(2)}) async-start(), calls=%async_computation.16 | async-start | bytes 1572864 | tf_op jit(solution)/shard_map/all_gather | solution.py:102
  (66 other events, 473.8 us)
Sparse Core Ops, SparseCore 0:
  77.1 19.9 all-gather.18
  102.7 25.8 all-gather.32
  130.4 21.4 all-gather.20
  153.6 22.8 all-gather.34
  178.1 20.9 all-gather.22
  200.8 17.8 all-gather.36
  220.5 16.1 all-gather.24
  238.6 19.0 all-gather.38
  259.5 19.9 all-gather.26
  281.1 18.7 all-gather.40
  301.7 16.3 all-gather.28
  319.7 36.2 all-gather.42
  363.2 22.9 all-gather.30
  388.7 27.5 all-gather.44
  420.3 15.8 all-gather.16
  502.7 38.3 all-gather.46
